TPU v7x, 32 devices: a whole 2x2x4 slice. The times are simulated.
32 devices in a mesh: lat: 4 (over x, core), lon: 2 (over y), lev: 4 (over z).
Axes of the slice: x: 2, y: 2, z: 4, core: 2. Of those that a mesh axis runs over, the one named last changes fastest.
Arguments:
- fields: float32 [2, 60, 128, 256], P(None, 'lev', 'lat', 'lon'), may hold values from -6 to 6
- diffusivity: float32 [60, 128, 256], P('lev', 'lat', 'lon'), may hold values from 0.02 to 0.24
- cloudy_index: int32 [4, 2048], P('lat', 'lon'), may hold values from 0 to 4095, as said below
- owners: int32 [4, 2048, 1], P('lat', 'lon'), may hold values from 0 to 1; in each aligned block of 256 rows (0 to 255, 256 to 511, ..., all dimensions but the last counted through in order) at most 256 rows name the same one
- w_in: bfloat16 [2, 120, 1024], P('lon'), may hold values from -0.5 to 0.5
- w_mid: bfloat16 [2, 2, 1024, 1024], P('lon'), may hold values from -0.1875 to 0.1875
- w_out: bfloat16 [2, 1024, 120], P('lon'), may hold values from -0.1875 to 0.1875
Outputs:
- fields_next: float32 [2, 60, 128, 256], P(None, 'lev', 'lat', 'lon')
Inputs may be any that keep to these rules, and one draw needn't show every extreme that they name: `cloudy_index`: in row i, entries j * 1024 to (j + 1) * 1024 - 1 are distinct column numbers a * 128 + b of the dycore block (i, j). `owners`: in each aligned block of 256 rows (one level slice of one dycore block), no regime is named by more than 256 rows.
All inputs are finite; a program needn't handle non-finite values.
Results may differ from a plain program's by a relative error of at most 0.00062.
Values may be sent and summed in bfloat16 or wider, within the bound.
No kernel may reach another device: no remote copies, remote signals or barrier semaphores. Data moves between devices by JAX's collectives and lax.ppermute only.
A program may use at most 64 MiB of HBM per device.

v0:
```python
import jax
import jax.numpy as jnp
from jax import lax
from jax.sharding import PartitionSpec as P

LEVELS = 60
STEPS = 3


def halo_exchange(cells, width):
    lat_count = lax.axis_size("lat")
    from_above = lax.ppermute(
        cells[..., cells.shape[-2] - width :, :], "lat", [(i, i + 1) for i in range(lat_count - 1)]
    )
    from_below = lax.ppermute(
        cells[..., :width, :], "lat", [(i + 1, i) for i in range(lat_count - 1)]
    )
    cells = jnp.concatenate([from_above, cells, from_below], axis=-2)
    lon_count = lax.axis_size("lon")
    left = cells[..., :width]
    right = cells[..., cells.shape[-1] - width :]
    if lon_count == 2:
        both = lax.ppermute(jnp.concatenate([right, left], axis=-1), "lon", [(0, 1), (1, 0)])
        from_left, from_right = (both[..., :width], both[..., width:])
    else:
        from_left = lax.ppermute(right, "lon", [(i, (i + 1) % lon_count) for i in range(lon_count)])
        from_right = lax.ppermute(left, "lon", [((i + 1) % lon_count, i) for i in range(lon_count)])
    return jnp.concatenate([from_left, cells, from_right], axis=-1)


def substep(values, coefficients):
    centre = values[..., 1:-1, 1:-1]
    middle = coefficients[:, 1:-1, 1:-1]
    updated = centre
    for lat_cut, lon_cut in (
        (slice(0, -2), slice(1, -1)),
        (slice(2, None), slice(1, -1)),
        (slice(1, -1), slice(0, -2)),
        (slice(1, -1), slice(2, None)),
    ):
        neighbour = values[..., lat_cut, lon_cut]
        face_coef = 0.5 * (middle + coefficients[:, lat_cut, lon_cut])
        updated = updated + face_coef * (neighbour - centre)
    return updated


def clear_outside(values, rim_width, lat_rows):
    lat_pos = (
        lax.axis_index("lat") * lat_rows - rim_width + jnp.arange(values.shape[-2], dtype=jnp.int32)
    )
    inside = (lat_pos >= 0) & (lat_pos < lat_rows * lax.axis_size("lat"))
    return jnp.where(inside[:, None], values, 0.0)


def dynamics(fields, diffusivity):
    kinds, level_rows, lat_rows, lon_cols = fields.shape
    stacked = jnp.concatenate(
        [fields.reshape(kinds * level_rows, lat_rows, lon_cols), diffusivity], axis=0
    )
    stacked = halo_exchange(stacked, STEPS)
    values = stacked[: kinds * level_rows].reshape(
        kinds, level_rows, lat_rows + 2 * STEPS, lon_cols + 2 * STEPS
    )
    kappa = stacked[kinds * level_rows :]
    for repeat in range(STEPS):
        trim = repeat
        coefficients = kappa[:, trim : kappa.shape[1] - trim, trim : kappa.shape[2] - trim]
        values = substep(values, coefficients)
        rim = STEPS - repeat - 1
        if rim:
            values = clear_outside(values, rim, lat_rows)
    return values


def network(features, w_first, w_middle, w_last):
    contract = (((0,), (0,)), ((), ()))
    hidden = jax.nn.gelu(
        lax.dot_general(w_first, features, contract, preferred_element_type=jnp.float32)
    ).astype(jnp.bfloat16)
    for layer_no in range(w_middle.shape[0]):
        hidden = jax.nn.gelu(
            lax.dot_general(
                w_middle[layer_no], hidden, contract, preferred_element_type=jnp.float32
            )
        ).astype(jnp.bfloat16)
    return lax.dot_general(w_last, hidden, contract, preferred_element_type=jnp.float32).astype(
        jnp.bfloat16
    )


def on_device(fields, diffusivity, cloudy_index, owners, w_in, w_mid, w_out):
    values = dynamics(fields, diffusivity)
    lev_count = lax.axis_size("lev")
    lon_count = lax.axis_size("lon")
    level_rows = values.shape[1]
    cells = values.shape[2] * values.shape[3]
    column_ids = cloudy_index[0]
    cloudy = column_ids.shape[0]
    per_device = cloudy // lev_count
    capacity = min(per_device, 4 * per_device // lon_count)
    feature_count = 2 * LEVELS
    lat_rows, lon_cols = (values.shape[2], values.shape[3])
    local_features = 2 * level_rows
    planes = values.reshape(local_features, lat_rows, lon_cols)
    row_of = column_ids // lon_cols
    col_of = column_ids % lon_cols
    col_picker = (jnp.arange(lon_cols, dtype=jnp.int32)[:, None] == col_of[None, :]).astype(
        jnp.bfloat16
    )
    row_match = jnp.arange(lat_rows, dtype=jnp.int32)[:, None] == row_of[None, :]
    by_row = jnp.dot(
        planes.astype(jnp.bfloat16).reshape(local_features * lat_rows, lon_cols),
        col_picker,
        preferred_element_type=jnp.bfloat16,
    ).reshape(local_features, lat_rows, cloudy)
    picked = jnp.sum(jnp.where(row_match[None], by_row, jnp.zeros_like(by_row)), axis=1)
    routes = owners[0, :, 0]
    group = lon_count * lev_count
    whole_slices = capacity == per_device
    if whole_slices:
        send_buffer = jnp.broadcast_to(
            picked.reshape(local_features, 1, lev_count, per_device),
            (local_features, lon_count, lev_count, per_device),
        ).reshape(local_features, group, capacity)
    else:
        pieces = routes.reshape(lev_count, per_device)
        onehot = (pieces[:, :, None] == jnp.arange(lon_count, dtype=jnp.int32)).astype(jnp.int32)
        slot_rank = jnp.sum(jnp.cumsum(onehot, 1) * onehot, 2) - 1
        piece_of = jnp.arange(lev_count, dtype=jnp.int32)[:, None]
        slot_index = ((pieces * lev_count + piece_of) * capacity + slot_rank).reshape(cloudy)
        send_buffer = (
            jnp.zeros((local_features, group * capacity), jnp.bfloat16)
            .at[:, slot_index]
            .set(picked)
            .reshape(local_features, group, capacity)
        )
    received = lax.all_to_all(send_buffer, ("lon", "lev"), split_axis=1, concat_axis=1, tiled=True)
    inputs = (
        received.reshape(2, level_rows, lon_count, lev_count, capacity)
        .transpose(0, 3, 1, 2, 4)
        .reshape(feature_count, lon_count * capacity)
    )
    outcome = network(inputs, w_in[0], w_mid[0], w_out[0])
    outgoing = (
        outcome.reshape(2, lev_count, level_rows, lon_count, capacity)
        .transpose(0, 2, 3, 1, 4)
        .reshape(local_features, group, capacity)
    )
    returned = lax.all_to_all(outgoing, ("lon", "lev"), split_axis=1, concat_axis=1, tiled=True)
    if whole_slices:
        returned = returned.reshape(local_features, lon_count, cloudy)
        tendency = returned[:, 0]
        for regime in range(1, lon_count):
            tendency = jnp.where(routes[None, :] == regime, returned[:, regime], tendency)
    else:
        tendency = returned.reshape(local_features, group * capacity)[:, slot_index]
    spread_rows = jnp.where(
        row_match[None], tendency[:, None, :], jnp.zeros_like(tendency)[:, None, :]
    )
    spread = lax.dot_general(
        spread_rows.reshape(local_features * lat_rows, cloudy),
        col_picker,
        (((1,), (1,)), ((), ())),
        preferred_element_type=jnp.float32,
    )
    updated = planes + spread.reshape(planes.shape)
    return updated.reshape(values.shape)


def solution(mesh):
    in_specs = (
        P(None, "lev", "lat", "lon"),
        P("lev", "lat", "lon"),
        P("lat", "lon"),
        P("lat", "lon", None),
        P("lon", None, None),
        P("lon", None, None, None),
        P("lon", None, None),
    )
    out_specs = P(None, "lev", "lat", "lon")
    return jax.shard_map(
        on_device, mesh=mesh, in_specs=in_specs, out_specs=out_specs, check_vma=False
    )
```

profile of v0, /device:TPU:0, one launch (start us, length us, event | category | flops | bytes accessed | tf_op | source)
XLA Modules:
  0.0 59.5 jit_solution(7515766200177670401)
XLA Ops:
  0.0 0.0 copy-start
  0.0 1.1 %pad_maximum_fusion.16 = (f32[45,3,128]{2,1,0:T(4,128)S(1)}, f32[45,3,128]{2,1,0:T(4,128)S(1)}) fusion(f32[15,32,128]{2,1,0:T(8,128)} %param.8, f32[30,32,128]{2,1,0:T(8,128)} %bitcast.69), kind=kLoop, calls=%fused_computation.140 | loop fusion | flops 34560 | bytes 875520 | tf_op jit(solution)/shard_map/slice | solution.py:13
  1.1 1.3 %collective-permute-start.1 = (f32[45,3,128]{2,1,0:T(4,128)S(1)}, f32[45,3,128]{2,1,0:T(4,128)S(1)}, u32[]{:S(2)}, u32[]{:S(2)}) collective-permute-start(f32[45,3,128]{2,1,0:T(4,128)S(1)} %get-tuple-element.24), channel_id=1, source_target_pairs={{8,0},{16,8},{24,16},{9,1},{17,9},{25,17},{10,2},{18,10},{26,18},{... | collective-permute-start | bytes 207368 | tf_op jit(solution)/shard_map/ppermute | solution.py:15
  2.4 3.0 %collective-permute-start = (f32[45,3,128]{2,1,0:T(4,128)S(1)}, f32[45,3,128]{2,1,0:T(4,128)S(1)}, u32[]{:S(2)}, u32[]{:S(2)}) collective-permute-start(f32[45,3,128]{2,1,0:T(4,128)S(1)} %get-tuple-element.23), channel_id=1, source_target_pairs={{0,8},{8,16},{16,24},{1,9},{9,17},{17,25},{2,10},{10,18},{18,26},{... | collective-permute-start | bytes 207368 | tf_op jit(solution)/shard_map/ppermute | solution.py:12
  5.5 0.7 %and_select_fusion = (s32[1,1024]{1,0:T(1,128)S(1)}, s32[1,1024]{1,0:T(1,128)S(1)}) fusion(s32[1,1024]{1,0:T(1,128)} %param.9), kind=kLoop, calls=%fused_computation.142 | loop fusion | flops 11264 | bytes 12288 | tf_op jit(solution)/shard_map/jit(remainder)/select_n | solution.py:106
  6.2 0.7 %and_select_fusion.1 = s32[1,1024]{1,0:T(1,128)S(1)} fusion(s32[1,1024]{1,0:T(1,128)S(1)} %get-tuple-element.6, s32[1,1024]{1,0:T(1,128)} %param.9), kind=kLoop, calls=%fused_computation.144 | loop fusion | flops 12288 | bytes 12288 | tf_op jit(solution)/shard_map/jit(floor_divide)/jit(_where)/select_n | solution.py:105
  6.9 0.0 collective-permute-done.1
  6.9 0.0 collective-permute-done
  6.9 1.3 %pad_maximum_fusion.1 = f32[45,38,128]{2,1,0:T(8,128)S(1)} fusion(f32[45,3,128]{2,1,0:T(4,128)S(1)} %collective-permute-done.1, f32[15,32,128]{2,1,0:T(8,128)} %param.8, f32[30,32,128]{2,1,0:T(8,128)} %bitcast.70, f32[45,3,128]{2,1,0:T(4,128)S(1)} %collective-permute-done), kind=kLoop, calls=%fused_computation.78 | loop fusion | flops 656640 | bytes 1751040 | tf_op jit(solution)/shard_map/concatenate | solution.py:18
  8.2 0.3 fusion.118
  8.5 0.4 copy.40
  8.9 0.0 copy-start.1
  8.9 0.0 copy-start.2
  9.0 0.4 copy.39
  9.4 3.0 %collective-permute-start.2 = (f32[45,38,6]{0,1,2:T(8,128)S(1)}, f32[45,38,6]{0,1,2:T(8,128)S(1)}, u32[]{:S(2)}, u32[]{:S(2)}) collective-permute-start(f32[45,38,6]{0,1,2:T(8,128)S(1)} %pad_maximum_fusion.14), channel_id=1, source_target_pairs={{0,4},{4,0},{1,5},{5,1},{2,6},{6,2},{3,7},{7,3},{8,12},{12,8},{9,1... | collective-permute-start | bytes 123128 | tf_op jit(solution)/shard_map/ppermute | solution.py:23
  12.5 3.5 %collective-permute-done.2 = f32[45,38,6]{0,1,2:T(8,128)S(1)} collective-permute-done((f32[45,38,6]{0,1,2:T(8,128)S(1)}, f32[45,38,6]{0,1,2:T(8,128)S(1)}, u32[]{:S(2)}, u32[]{:S(2)}) %collective-permute-start.2) | collective-permute-done | bytes 41072 | tf_op jit(solution)/shard_map/ppermute | solution.py:23
  16.0 0.5 copy.52
  16.4 0.5 copy.51
  16.9 0.0 copy-done.1
  16.9 0.0 copy-done.2
  16.9 1.0 %pad_maximum_fusion = f32[45,38,134]{2,1,0:T(8,128)S(1)} fusion(f32[45,38,3]{2,1,0:T(8,128)S(1)} %copy.52, f32[45,3,128]{2,1,0:T(4,128)S(1)} %collective-permute-done.1, f32[15,32,128]{2,1,0:T(8,128)S(1)} %copy-done.2, f32[30,32,128]{2,1,0:T(8,128)S(1)} %bitcast.71, f32[45,3,128]{2,1,0:T(4,128)S(1)} %collective-permute-done, f32[45,38,3]{2,1,0:T(8,128)S(1)} %copy.51), kind=kLoop, calls=%fused_computation.37 | loop fusion | flops 1145700 | bytes 1833120 | tf_op jit(solution)/shard_map/concatenate | solution.py:28
  17.9 0.1 slice.196
  18.0 0.7 %fusion.84 = (f32[15,36,132]{2,1,0:T(8,128)S(1)}, f32[15,36,132]{2,1,0:T(8,128)S(1)}, f32[15,36,132]{2,1,0:T(8,128)S(1)}, f32[15,36,132]{2,1,0:T(8,128)S(1)}) fusion(f32[45,38,134]{2,1,0:T(8,128)S(1)} %pad_maximum_fusion), kind=kLoop, calls=%fused_computation.94 | loop fusion | flops 570240 | bytes 2566080 | tf_op jit(solution)/shard_map/mul | solution.py:42
  18.7 1.4 %fusion.44 = f32[2,15,36,132]{3,2,1,0:T(8,128)S(1)} fusion(f32[2,15,38,134]{3,2,1,0:T(8,128)S(1)} %bitcast.68, f32[15,36,132]{2,1,0:T(8,128)S(1)} %get-tuple-element.14, f32[15,36,132]{2,1,0:T(8,128)S(1)} %get-tuple-element.15, f32[15,36,132]{2,1,0:T(8,128)S(1)} %get-tuple-element.16, f32[15,36,132]{2,1,0:T(8,128)S(1)} %get-tuple-element.13, ...), kind=kLoop, calls=%fused_computation.54 | loop fusion | flops 1853280 | bytes 4561956 | tf_op jit(solution)/shard_map/jit(_where)/select_n | solution.py:52
  20.1 0.9 %fusion.80 = (f32[15,34,130]{2,1,0:T(8,128)S(1)}, f32[15,34,130]{2,1,0:T(8,128)S(1)}, f32[15,34,130]{2,1,0:T(8,128)S(1)}, f32[15,34,130]{2,1,0:T(8,128)S(1)}) fusion(f32[45,38,134]{2,1,0:T(8,128)S(1)} %pad_maximum_fusion, f32[45,38,3]{2,1,0:T(8,128)S(1)} %copy.52, f32[45,3,128]{2,1,0:T(4,128)S(1)} %collective-permute-done.1, ...), kind=kLoop, calls=%fused_computation.86 | loop fusion | flops 1060800 | bytes 2772960 | tf_op jit(solution)/shard_map/mul | solution.py:42
  21.0 1.4 %fusion.35 = f32[2,15,34,130]{3,2,1,0:T(8,128)S(1)} fusion(f32[2,15,36,132]{3,2,1,0:T(8,128)S(1)} %fusion.44, f32[15,34,130]{2,1,0:T(8,128)S(1)} %get-tuple-element.11, f32[15,34,130]{2,1,0:T(8,128)S(1)} %get-tuple-element.12, f32[15,34,130]{2,1,0:T(8,128)S(1)} %get-tuple-element.10, f32[15,34,130]{2,1,0:T(8,128)S(1)} %get-tuple-element.9, ...), kind=kLoop, calls=%fused_computation.41 | loop fusion | flops 1723800 | bytes 4243234 | tf_op jit(solution)/shard_map/jit(_where)/select_n | solution.py:52
  22.4 0.4 fusion.101
  22.8 0.6 %fusion.89 = f32[2,15,32,128]{3,2,1,0:T(8,128)S(1)} fusion(f32[2,15,34,130]{3,2,1,0:T(8,128)S(1)} %fusion.35, f32[15,32,128]{2,1,0:T(8,128)S(1)} %get-tuple-element.18, f32[15,32,128]{2,1,0:T(8,128)S(1)} %get-tuple-element.17, f32[15,32,128]{2,1,0:T(8,128)S(1)} %get-tuple-element.22, f32[15,32,128]{2,1,0:T(8,128)S(1)} %get-tuple-element.21), kind=kLoop, calls=%fused_computation.99 | loop fusion | flops 1474560 | bytes 3932160 | tf_op jit(solution)/shard_map/add | solution.py:43
  23.4 0.7 %select_reduce_fusion = bf16[30,1024]{1,0:T(8,128)(2,1)S(1)} fusion(pred[32,1024]{1,0:T(8,128)(4,1)S(1)} %iota_compare_fusion.1, bf16[30,32,128]{2,1,0:T(8,128)(2,1)S(1)} %bitcast_convert_fusion, s32[1024]{0:T(1024)S(1)} %bitcast.82), kind=kOutput, calls=%fused_computation.35 | convolution fusion | flops 253724672 | bytes 344064 | tf_op jit(solution)/shard_map/dot_general | solution.py:111
  24.2 14.3 %all_to_all.10 = bf16[30,8,256]{2,0,1:T(8,128)(2,1)S(1)} all-to-all(bf16[30,8,256]{2,0,1:T(8,128)(2,1)S(1)} %bitcast.75), channel_id=1, replica_groups=mesh['lat'=4,'lon'=2,'lev'=4] {'lon','lev'}, dimensions={1} | all-to-all | bytes 245760 | tf_op jit(solution)/shard_map/all_to_all | solution.py:137
  38.5 0.1 copy.57
  38.6 0.1 copy.45
  38.8 0.0 copy-done
  38.8 0.0 copy-start.4
  38.8 3.7 %fusion.15 = bf16[1024,512]{0,1:T(8,128)(2,1)S(1)} fusion(bf16[1,2,1024,1024]{3,2,1,0:T(8,128)(2,1)} %param.12, bf16[120,512]{1,0:T(8,128)(2,1)S(1)} %bitcast.79, bf16[1,120,1024]{2,1,0:T(8,128)(2,1)S(1)} %copy-done), kind=kOutput, calls=%fused_computation.18 | convolution fusion | flops 1209008128 | bytes 3514368 | tf_op jit(solution)/shard_map/dot_general | solution.py:82
  42.5 0.0 copy-done.4
  42.5 0.0 copy-start.3
  42.5 3.4 %fusion.64 = bf16[120,512]{1,0:T(8,128)(2,1)S(1)} fusion(bf16[1024,512]{0,1:T(8,128)(2,1)S(1)} %fusion.15, bf16[1,2,1024,1024]{3,2,1,0:T(8,128)(2,1)} %param.12, bf16[1,1024,120]{1,2,0:T(8,128)(2,1)S(1)} %copy-done.4), kind=kOutput, calls=%fused_computation.67 | convolution fusion | flops 1204350976 | bytes 3514368 | tf_op jit(solution)/shard_map/dot_general | solution.py:86
  46.1 0.7 %copy.47 = bf16[30,8,256]{2,0,1:T(8,128)(2,1)} copy(bf16[30,8,256]{2,1,0:T(8,128)(2,1)S(1)} %reshape.103) | data formatting | bytes 245760 | tf_op jit(solution)/shard_map/reshape | solution.py:147
  46.8 3.4 %all-to-all-start.1 = ((bf16[30,8,256]{2,0,1:T(8,128)(2,1)}), bf16[30,8,256]{2,0,1:T(8,128)(2,1)S(1)}, u32[]{:S(2)}, u32[]{:S(2)}) async-start(bf16[30,8,256]{2,0,1:T(8,128)(2,1)} %copy.47), calls=%async_computation.1 | async-start | bytes 262144 | tf_op jit(solution)/shard_map/all_to_all | solution.py:149
  50.2 0.0 copy-done.3
  50.2 7.4 %all-to-all-done.1 = bf16[30,8,256]{2,0,1:T(8,128)(2,1)S(1)} async-done(((bf16[30,8,256]{2,0,1:T(8,128)(2,1)}), bf16[30,8,256]{2,0,1:T(8,128)(2,1)S(1)}, u32[]{:S(2)}, u32[]{:S(2)}) %all-to-all-start.1) | async-done | bytes 122912 | tf_op jit(solution)/shard_map/all_to_all | solution.py:149
  57.6 0.1 copy.48
  57.7 0.1 reshape.104
  57.8 0.2 broadcast_select_fusion
  58.0 1.5 %fusion.51 = f32[30,32,128]{2,1,0:T(8,128)} fusion(f32[30,32,128]{2,1,0:T(8,128)S(1)} %bitcast.74, pred[32,1024]{1,0:T(8,128)(4,1)S(1)} %iota_compare_fusion.1, bf16[30,1024]{1,0:T(8,128)(2,1)S(1)} %bitcast.80, s32[1024]{0:T(1024)S(1)} %bitcast.83), kind=kOutput, calls=%fused_computation.64 | convolution fusion | flops 252895232 | bytes 1081344 | tf_op jit(solution)/shard_map/dot_general | solution.py:160
  (16 shorter events, 0.4 us)
Async XLA Ops:
  0.0 38.8 %copy-start = (bf16[1,120,1024]{2,1,0:T(8,128)(2,1)S(1)}, bf16[1,120,1024]{2,1,0:T(8,128)(2,1)}, u32[]{:S(2)}) copy-start(bf16[1,120,1024]{2,1,0:T(8,128)(2,1)} %param.11) | copy-start | bytes 737284
  1.1 5.8 %collective-permute-start.1 = (f32[45,3,128]{2,1,0:T(4,128)S(1)}, f32[45,3,128]{2,1,0:T(4,128)S(1)}, u32[]{:S(2)}, u32[]{:S(2)}) collective-permute-start(f32[45,3,128]{2,1,0:T(4,128)S(1)} %get-tuple-element.24), channel_id=1, source_target_pairs={{8,0},{16,8},{24,16},{9,1},{17,9},{25,17},{10,2},{18,10},{26,18},{... | collective-permute-start | bytes 207368 | tf_op jit(solution)/shard_map/ppermute | solution.py:15
  2.4 4.5 %collective-permute-start = (f32[45,3,128]{2,1,0:T(4,128)S(1)}, f32[45,3,128]{2,1,0:T(4,128)S(1)}, u32[]{:S(2)}, u32[]{:S(2)}) collective-permute-start(f32[45,3,128]{2,1,0:T(4,128)S(1)} %get-tuple-element.23), channel_id=1, source_target_pairs={{0,8},{8,16},{16,24},{1,9},{9,17},{17,25},{2,10},{10,18},{18,26},{... | collective-permute-start | bytes 207368 | tf_op jit(solution)/shard_map/ppermute | solution.py:12
  8.9 8.0 %copy-start.1 = (f32[2,15,32,128]{3,2,1,0:T(8,128)S(1)}, f32[2,15,32,128]{3,2,1,0:T(8,128)}, u32[]{:S(2)}) copy-start(f32[2,15,32,128]{3,2,1,0:T(8,128)} %param.7) | copy-start | bytes 1474564
  8.9 8.0 %copy-start.2 = (f32[15,32,128]{2,1,0:T(8,128)S(1)}, f32[15,32,128]{2,1,0:T(8,128)}, u32[]{:S(2)}) copy-start(f32[15,32,128]{2,1,0:T(8,128)} %param.8) | copy-start | bytes 737284
  9.4 6.6 %collective-permute-start.2 = (f32[45,38,6]{0,1,2:T(8,128)S(1)}, f32[45,38,6]{0,1,2:T(8,128)S(1)}, u32[]{:S(2)}, u32[]{:S(2)}) collective-permute-start(f32[45,38,6]{0,1,2:T(8,128)S(1)} %pad_maximum_fusion.14), channel_id=1, source_target_pairs={{0,4},{4,0},{1,5},{5,1},{2,6},{6,2},{3,7},{7,3},{8,12},{12,8},{9,1... | collective-permute-start | bytes 123128 | tf_op jit(solution)/shard_map/ppermute | solution.py:23
  38.8 3.8 %copy-start.4 = (bf16[1,1024,120]{1,2,0:T(8,128)(2,1)S(1)}, bf16[1,1024,120]{1,2,0:T(8,128)(2,1)}, u32[]{:S(2)}) copy-start(bf16[1,1024,120]{1,2,0:T(8,128)(2,1)} %param.13) | copy-start | bytes 737284
  42.5 7.7 %copy-start.3 = (s32[1,1024,1]{1,2,0:T(1,128)S(1)}, s32[1,1024,1]{1,2,0:T(1,128)}, u32[]{:S(2)}) copy-start(s32[1,1024,1]{1,2,0:T(1,128)} %param.10) | copy-start | bytes 12292
  46.8 10.8 %all-to-all-start.1 = ((bf16[30,8,256]{2,0,1:T(8,128)(2,1)}), bf16[30,8,256]{2,0,1:T(8,128)(2,1)S(1)}, u32[]{:S(2)}, u32[]{:S(2)}) async-start(bf16[30,8,256]{2,0,1:T(8,128)(2,1)} %copy.47), calls=%async_computation.1 | async-start | bytes 262144 | tf_op jit(solution)/shard_map/all_to_all | solution.py:149
where the time goes:
time: 60 us; the launch traced here: 59.5 us
  blocking collectives  14.3 us (24%)
  waiting for transfers between devices  10.9 us (18%)
  starting transfers between devices  10.7 us (18%)
  other arithmetic  10.5 us (18%)
  matrix products  9.36 us (16%)
  local copies, waits for them, and re-layouts  3.44 us (6%)
    all_to_all x1, blocking collectives, on_device(): lax.all_to_all(send_buffer, ('lon', 'lev'), split_axis=1, concat_axis=1,...  14.3 us
    all_to_all x1, waiting for transfers between devices, on_device(): lax.all_to_all(outgoing, ('lon', 'lev'), split_axis=1, concat_axis=1, til...  7.42 us
    dot_general x1, matrix products, network(): lax.dot_general(w_middle[layer_no], hidden, contract, preferred_element_t...  3.73 us
    ppermute x1, waiting for transfers between devices, halo_exchange(): lax.ppermute(jnp.concatenate([right, left], axis=-1), 'lon', [(0, 1), (1,...  3.51 us
    dot_general x1, matrix products, network(): lax.dot_general(w_last, hidden, contract, preferred_element_type=jnp.floa...  3.44 us
    all_to_all x1, starting transfers between devices, on_device(): lax.all_to_all(outgoing, ('lon', 'lev'), split_axis=1, concat_axis=1, til...  3.37 us
    ppermute x1, starting transfers between devices, halo_exchange(): lax.ppermute(cells[..., cells.shape[-2] - width:, :], 'lat', [(i, i + 1)...  3.04 us
    ppermute x1, starting transfers between devices, halo_exchange(): lax.ppermute(jnp.concatenate([right, left], axis=-1), 'lon', [(0, 1), (1,...  3.03 us
  transfers between devices with their start and end apart: 4, of which 2 were waited for; matrix products, arithmetic and copies ran while one was open for 2% of the time, Pallas kernels for 0%

commit v1 on v0

--- a/solution.py
+++ b/solution.py
@@ -5,6 +5,17 @@
 
 LEVELS = 60
 STEPS = 3
+
+
+def cut_along(x, dim, size):
+    before, after = (x.shape[:dim], x.shape[dim + 1 :])
+    return jnp.moveaxis(x.reshape(*before, size, -1, *after), dim, 0)
+
+
+def laid_out(blocks, dim):
+    lengths = list(blocks.shape[1:])
+    lengths[dim] *= blocks.shape[0]
+    return jnp.moveaxis(blocks, 0, dim).reshape(lengths)
 
 
 def halo_exchange(cells, width):
@@ -146,7 +157,16 @@
         .transpose(0, 2, 3, 1, 4)
         .reshape(local_features, group, capacity)
     )
-    returned = lax.all_to_all(outgoing, ("lon", "lev"), split_axis=1, concat_axis=1, tiled=True)
+    devices, index = (lax.axis_size(("lon", "lev")), lax.axis_index(("lon", "lev")))
+    pieces_2 = cut_along(outgoing, 1, devices)
+    outs = [pieces_2[index]]
+    for step in range(1, devices):
+        sent = pieces_2[index ^ step]
+        outs.append(
+            lax.ppermute(sent, ("lon", "lev"), [(i_2, i_2 ^ step) for i_2 in range(devices)])
+        )
+    pieces_2 = jnp.stack(outs)[index ^ jnp.arange(devices)]
+    returned = laid_out(pieces_2, 1)
     if whole_slices:
         returned = returned.reshape(local_features, lon_count, cloudy)
         tendency = returned[:, 0]

time: 60 us -> 64 us (1.067)
  starting transfers between devices: 10.7 us -> 25.5 us
  blocking collectives: 14.3 us -> 0 us
  waiting for transfers between devices: 10.9 us -> 13.5 us
  local copies, waits for them, and re-layouts: 3.44 us -> 4.34 us
    all_to_all x1 -> x0, blocking collectives: 14.3 us -> none  [on_device(): lax.all_to_all(send_buffer, ('lon', 'lev'), split_axis=1, concat_axis=1,...]
    ppermute x0 -> x7, starting transfers between devices: none -> 11.3 us  [on_device(): lax.ppermute(sent, ('lon', 'lev'), [(i_2, i_2 ^ step) for i_2 in range(de...]
    all_to_all x1, starting transfers between devices: 3.37 us -> 6.79 us  [on_device(): lax.all_to_all(send_buffer, ('lon', 'lev'), split_axis=1, concat_axis=1,...]
    ppermute x0 -> x7, waiting for transfers between devices: none -> 2.33 us  [on_device(): lax.ppermute(sent, ('lon', 'lev'), [(i_2, i_2 ^ step) for i_2 in range(de...]
    reshape x3 -> x0, local copies, waits for them, and re-layouts: 0.77 us -> none  [the longest x2 0.72 us: on_device(): outgoing = outcome.reshape(2, lev_count, level_rows, lon_count, capacity)...]
    broadcast_in_dim x3, local copies, waits for them, and re-layouts: 0.05 us -> 0.71 us  [on_device(): jnp.broadcast_to(picked.reshape(local_features, 1, lev_count, per_device)...]
  transfers between devices with their start and end apart: 4 -> 11, of which waited for: 2 -> 3; matrix products, arithmetic and copies ran while one was open for 2% -> 2% of each run, Pallas kernels for 0% -> 0%
where the time goes in v1:
time: 64 us; the launch traced here: 63.6 us
  starting transfers between devices  25.5 us (40%)
  waiting for transfers between devices  13.5 us (21%)
  other arithmetic  10.5 us (16%)
  matrix products  9.39 us (15%)
  local copies, waits for them, and re-layouts  4.34 us (7%)
    ppermute x7, starting transfers between devices, on_device(): lax.ppermute(sent, ('lon', 'lev'), [(i_2, i_2 ^ step) for i_2 in range(de...  11.3 us
    all_to_all x1, waiting for transfers between devices, on_device(): lax.all_to_all(send_buffer, ('lon', 'lev'), split_axis=1, concat_axis=1,...  7.63 us
    all_to_all x1, starting transfers between devices, on_device(): lax.all_to_all(send_buffer, ('lon', 'lev'), split_axis=1, concat_axis=1,...  6.79 us
    dot_general x1, matrix products, network(): lax.dot_general(w_middle[layer_no], hidden, contract, preferred_element_t...  3.73 us
    ppermute x1, waiting for transfers between devices, halo_exchange(): lax.ppermute(jnp.concatenate([right, left], axis=-1), 'lon', [(0, 1), (1,...  3.54 us
    dot_general x1, matrix products, network(): lax.dot_general(w_last, hidden, contract, preferred_element_type=jnp.floa...  3.48 us
    ppermute x1, starting transfers between devices, halo_exchange(): lax.ppermute(cells[..., cells.shape[-2] - width:, :], 'lat', [(i, i + 1)...  3.04 us
    ppermute x1, starting transfers between devices, halo_exchange(): lax.ppermute(jnp.concatenate([right, left], axis=-1), 'lon', [(0, 1), (1,...  3.03 us
  transfers between devices with their start and end apart: 11, of which 3 were waited for; matrix products, arithmetic and copies ran while one was open for 2% of the time, Pallas kernels for 0%

profile of v1, /device:TPU:0, one launch (start us, length us, event | category | flops | bytes accessed | tf_op | source)
XLA Modules:
  0.0 63.6 jit_solution(18341215589337476342)
XLA Ops:
  0.0 1.1 %pad_maximum_fusion.16 = (f32[45,3,128]{2,1,0:T(4,128)S(1)}, f32[45,3,128]{2,1,0:T(4,128)S(1)}) fusion(f32[15,32,128]{2,1,0:T(8,128)} %param.8, f32[30,32,128]{2,1,0:T(8,128)} %bitcast.116), kind=kLoop, calls=%fused_computation.141 | loop fusion | flops 34560 | bytes 875520 | tf_op jit(solution)/shard_map/slice | solution.py:24
  1.1 1.3 %collective-permute-start.1 = (f32[45,3,128]{2,1,0:T(4,128)S(1)}, f32[45,3,128]{2,1,0:T(4,128)S(1)}, u32[]{:S(2)}, u32[]{:S(2)}) collective-permute-start(f32[45,3,128]{2,1,0:T(4,128)S(1)} %get-tuple-element.24), channel_id=1, source_target_pairs={{8,0},{16,8},{24,16},{9,1},{17,9},{25,17},{10,2},{18,10},{26,18},{... | collective-permute-start | bytes 207368 | tf_op jit(solution)/shard_map/ppermute | solution.py:26
  2.4 3.0 %collective-permute-start = (f32[45,3,128]{2,1,0:T(4,128)S(1)}, f32[45,3,128]{2,1,0:T(4,128)S(1)}, u32[]{:S(2)}, u32[]{:S(2)}) collective-permute-start(f32[45,3,128]{2,1,0:T(4,128)S(1)} %get-tuple-element.23), channel_id=1, source_target_pairs={{0,8},{8,16},{16,24},{1,9},{9,17},{17,25},{2,10},{10,18},{18,26},{... | collective-permute-start | bytes 207368 | tf_op jit(solution)/shard_map/ppermute | solution.py:23
  5.5 0.7 %and_select_fusion = (s32[1,1024]{1,0:T(1,128)S(1)}, s32[1,1024]{1,0:T(1,128)S(1)}) fusion(s32[1,1024]{1,0:T(1,128)} %param.9), kind=kLoop, calls=%fused_computation.158 | loop fusion | flops 11264 | bytes 12288 | tf_op jit(solution)/shard_map/jit(remainder)/select_n | solution.py:117
  6.2 0.7 %and_select_fusion.1 = s32[1,1024]{1,0:T(1,128)S(1)} fusion(s32[1,1024]{1,0:T(1,128)S(1)} %get-tuple-element.6, s32[1,1024]{1,0:T(1,128)} %param.9), kind=kLoop, calls=%fused_computation.160 | loop fusion | flops 12288 | bytes 12288 | tf_op jit(solution)/shard_map/jit(floor_divide)/jit(_where)/select_n | solution.py:116
  7.0 0.0 collective-permute-done
  7.0 1.3 %pad_maximum_fusion.1 = f32[45,38,128]{2,1,0:T(8,128)S(1)} fusion(f32[45,3,128]{2,1,0:T(4,128)S(1)} %collective-permute-done.1, f32[15,32,128]{2,1,0:T(8,128)} %param.8, f32[30,32,128]{2,1,0:T(8,128)} %bitcast.117, f32[45,3,128]{2,1,0:T(4,128)S(1)} %collective-permute-done), kind=kLoop, calls=%fused_computation.79 | loop fusion | flops 656640 | bytes 1751040 | tf_op jit(solution)/shard_map/concatenate | solution.py:29
  8.2 0.3 fusion.119
  8.5 0.4 copy.41
  9.0 0.4 copy.40
  9.5 3.0 %collective-permute-start.2 = (f32[45,38,6]{0,1,2:T(8,128)S(1)}, f32[45,38,6]{0,1,2:T(8,128)S(1)}, u32[]{:S(2)}, u32[]{:S(2)}) collective-permute-start(f32[45,38,6]{0,1,2:T(8,128)S(1)} %pad_maximum_fusion.14), channel_id=1, source_target_pairs={{0,4},{4,0},{1,5},{5,1},{2,6},{6,2},{3,7},{7,3},{8,12},{12,8},{9,1... | collective-permute-start | bytes 123128 | tf_op jit(solution)/shard_map/ppermute | solution.py:34
  12.5 3.5 %collective-permute-done.2 = f32[45,38,6]{0,1,2:T(8,128)S(1)} collective-permute-done((f32[45,38,6]{0,1,2:T(8,128)S(1)}, f32[45,38,6]{0,1,2:T(8,128)S(1)}, u32[]{:S(2)}, u32[]{:S(2)}) %collective-permute-start.2) | collective-permute-done | bytes 41072 | tf_op jit(solution)/shard_map/ppermute | solution.py:34
  16.0 0.5 copy.60
  16.5 0.5 copy.59
  17.0 1.0 %pad_maximum_fusion = f32[45,38,134]{2,1,0:T(8,128)S(1)} fusion(f32[45,38,3]{2,1,0:T(8,128)S(1)} %copy.60, f32[45,3,128]{2,1,0:T(4,128)S(1)} %collective-permute-done.1, f32[15,32,128]{2,1,0:T(8,128)S(1)} %copy-done.2, f32[30,32,128]{2,1,0:T(8,128)S(1)} %bitcast.118, f32[45,3,128]{2,1,0:T(4,128)S(1)} %collective-permute-done, f32[45,38,3]{2,1,0:T(8,128)S(1)} %copy.59), kind=kLoop, calls=%fused_computation.38 | loop fusion | flops 1145700 | bytes 1833120 | tf_op jit(solution)/shard_map/concatenate | solution.py:39
  18.0 0.1 slice.198
  18.1 0.7 %fusion.84 = (f32[15,36,132]{2,1,0:T(8,128)S(1)}, f32[15,36,132]{2,1,0:T(8,128)S(1)}, f32[15,36,132]{2,1,0:T(8,128)S(1)}, f32[15,36,132]{2,1,0:T(8,128)S(1)}) fusion(f32[45,38,134]{2,1,0:T(8,128)S(1)} %pad_maximum_fusion), kind=kLoop, calls=%fused_computation.95 | loop fusion | flops 570240 | bytes 2566080 | tf_op jit(solution)/shard_map/mul | solution.py:53
  18.8 1.4 %fusion.44 = f32[2,15,36,132]{3,2,1,0:T(8,128)S(1)} fusion(f32[2,15,38,134]{3,2,1,0:T(8,128)S(1)} %bitcast.115, f32[15,36,132]{2,1,0:T(8,128)S(1)} %get-tuple-element.14, f32[15,36,132]{2,1,0:T(8,128)S(1)} %get-tuple-element.15, f32[15,36,132]{2,1,0:T(8,128)S(1)} %get-tuple-element.16, f32[15,36,132]{2,1,0:T(8,128)S(1)} %get-tuple-element.13, ...), kind=kLoop, calls=%fused_computation.55 | loop fusion | flops 1853280 | bytes 4561956 | tf_op jit(solution)/shard_map/jit(_where)/select_n | solution.py:63
  20.2 0.9 %fusion.80 = (f32[15,34,130]{2,1,0:T(8,128)S(1)}, f32[15,34,130]{2,1,0:T(8,128)S(1)}, f32[15,34,130]{2,1,0:T(8,128)S(1)}, f32[15,34,130]{2,1,0:T(8,128)S(1)}) fusion(f32[45,38,134]{2,1,0:T(8,128)S(1)} %pad_maximum_fusion, f32[45,38,3]{2,1,0:T(8,128)S(1)} %copy.60, f32[45,3,128]{2,1,0:T(4,128)S(1)} %collective-permute-done.1, ...), kind=kLoop, calls=%fused_computation.87 | loop fusion | flops 1060800 | bytes 2772960 | tf_op jit(solution)/shard_map/mul | solution.py:53
  21.1 1.4 %fusion.35 = f32[2,15,34,130]{3,2,1,0:T(8,128)S(1)} fusion(f32[2,15,36,132]{3,2,1,0:T(8,128)S(1)} %fusion.44, f32[15,34,130]{2,1,0:T(8,128)S(1)} %get-tuple-element.11, f32[15,34,130]{2,1,0:T(8,128)S(1)} %get-tuple-element.12, f32[15,34,130]{2,1,0:T(8,128)S(1)} %get-tuple-element.10, f32[15,34,130]{2,1,0:T(8,128)S(1)} %get-tuple-element.9, ...), kind=kLoop, calls=%fused_computation.42 | loop fusion | flops 1723800 | bytes 4243234 | tf_op jit(solution)/shard_map/jit(_where)/select_n | solution.py:63
  22.5 0.4 fusion.101
  22.9 0.6 fusion.89
  23.5 0.0 copy-start.3
  23.5 0.7 %select_reduce_fusion = bf16[30,1024]{1,0:T(8,128)(2,1)S(1)} fusion(pred[32,1024]{1,0:T(8,128)(4,1)S(1)} %iota_compare_fusion.1, bf16[30,32,128]{2,1,0:T(8,128)(2,1)S(1)} %bitcast_convert_fusion, s32[1024]{0:T(1024)S(1)} %bitcast.137), kind=kOutput, calls=%fused_computation.36 | convolution fusion | flops 253724672 | bytes 344064 | tf_op jit(solution)/shard_map/dot_general | solution.py:122
  24.3 0.7 %broadcast_in_dim.102 = bf16[30,2,4,256]{3,0,2,1:T(8,128)(2,1)} broadcast(bf16[30,4,256]{2,0,1:T(8,128)(2,1)S(1)} %copy.44), dimensions={0,2,3} | broadcast | bytes 184320 | tf_op jit(solution)/shard_map/broadcast_in_dim | solution.py:132
  25.0 6.8 %all-to-all-start = ((bf16[30,8,256]{2,0,1:T(8,128)(2,1)}), bf16[30,8,256]{2,0,1:T(8,128)(2,1)S(1)}, u32[]{:S(2)}, u32[]{:S(2)}) async-start(bf16[30,8,256]{2,0,1:T(8,128)(2,1)} %bitcast.6), calls=%async_computation | async-start | bytes 262144 | tf_op jit(solution)/shard_map/all_to_all | solution.py:148
  31.8 7.6 %all-to-all-done = bf16[30,8,256]{2,0,1:T(8,128)(2,1)S(1)} async-done(((bf16[30,8,256]{2,0,1:T(8,128)(2,1)}), bf16[30,8,256]{2,0,1:T(8,128)(2,1)S(1)}, u32[]{:S(2)}, u32[]{:S(2)}) %all-to-all-start) | async-done | bytes 122912 | tf_op jit(solution)/shard_map/all_to_all | solution.py:148
  39.5 0.1 copy.73
  39.6 0.1 copy.46
  39.7 0.0 copy-start.4
  39.7 3.7 %fusion.15 = bf16[1024,512]{0,1:T(8,128)(2,1)S(1)} fusion(bf16[1,2,1024,1024]{3,2,1,0:T(8,128)(2,1)} %param.12, bf16[120,512]{1,0:T(8,128)(2,1)S(1)} %bitcast.127, bf16[1,120,1024]{2,1,0:T(8,128)(2,1)S(1)} %copy-done), kind=kOutput, calls=%fused_computation.19 | convolution fusion | flops 1209008128 | bytes 3514368 | tf_op jit(solution)/shard_map/dot_general | solution.py:93
  43.5 3.5 %fusion.64 = bf16[120,512]{1,0:T(8,128)(2,1)S(1)} fusion(bf16[1024,512]{0,1:T(8,128)(2,1)S(1)} %fusion.15, bf16[1,2,1024,1024]{3,2,1,0:T(8,128)(2,1)} %param.12, bf16[1,1024,120]{1,2,0:T(8,128)(2,1)S(1)} %copy-done.4), kind=kOutput, calls=%fused_computation.68 | convolution fusion | flops 1204350976 | bytes 3514368 | tf_op jit(solution)/shard_map/dot_general | solution.py:97
  47.1 0.3 constant_dynamic-slice_fusion
  47.4 0.1 collective-permute-start.3
  47.5 1.0 %collective-permute-start.4 = (bf16[30,1,256]{2,0,1:T(8,128)(2,1)S(1)}, bf16[30,1,256]{2,0,1:T(8,128)(2,1)S(1)}, u32[]{:S(2)}, u32[]{:S(2)}) collective-permute-start(bf16[30,1,256]{2,0,1:T(8,128)(2,1)S(1)} %bitcast.134), channel_id=1, source_target_pairs={{0,2},{1,3},{2,0},{3,1},{4,6},{5,7},{6,4},{7,5},{8,10},{9,11},{10,... | collective-permute-start | bytes 46088 | tf_op jit(solution)/shard_map/ppermute | solution.py:166
  48.5 3.4 %collective-permute-start.5 = (bf16[30,1,256]{2,0,1:T(8,128)(2,1)S(1)}, bf16[30,1,256]{2,0,1:T(8,128)(2,1)S(1)}, u32[]{:S(2)}, u32[]{:S(2)}) collective-permute-start(bf16[30,1,256]{2,0,1:T(8,128)(2,1)S(1)} %bitcast.133), channel_id=1, source_target_pairs={{0,3},{1,2},{2,1},{3,0},{4,7},{5,6},{6,5},{7,4},{8,11},{9,10},{10,... | collective-permute-start | bytes 46088 | tf_op jit(solution)/shard_map/ppermute | solution.py:166
  51.9 0.6 collective-permute-start.6
  52.5 0.1 collective-permute-start.7
  52.6 0.0 collective-permute-done.3
  52.6 2.1 %collective-permute-start.8 = (bf16[30,1,256]{2,0,1:T(8,128)(2,1)S(1)}, bf16[30,1,256]{2,0,1:T(8,128)(2,1)S(1)}, u32[]{:S(2)}, u32[]{:S(2)}) collective-permute-start(bf16[30,1,256]{2,0,1:T(8,128)(2,1)S(1)} %bitcast.130), channel_id=1, source_target_pairs={{0,6},{1,7},{2,4},{3,5},{4,2},{5,3},{6,0},{7,1},{8,14},{9,15},{10,... | collective-permute-start | bytes 46088 | tf_op jit(solution)/shard_map/ppermute | solution.py:166
  54.8 4.0 %collective-permute-start.9 = (bf16[30,1,256]{2,0,1:T(8,128)(2,1)S(1)}, bf16[30,1,256]{2,0,1:T(8,128)(2,1)S(1)}, u32[]{:S(2)}, u32[]{:S(2)}) collective-permute-start(bf16[30,1,256]{2,0,1:T(8,128)(2,1)S(1)} %bitcast.129), channel_id=1, source_target_pairs={{0,7},{1,6},{2,5},{3,4},{4,3},{5,2},{6,1},{7,0},{8,15},{9,14},{10,... | collective-permute-start | bytes 46088 | tf_op jit(solution)/shard_map/ppermute | solution.py:166
  58.8 0.0 collective-permute-done.5
  58.9 2.3 %collective-permute-done.9 = bf16[30,1,256]{2,0,1:T(8,128)(2,1)S(1)} collective-permute-done((bf16[30,1,256]{2,0,1:T(8,128)(2,1)S(1)}, bf16[30,1,256]{2,0,1:T(8,128)(2,1)S(1)}, u32[]{:S(2)}, u32[]{:S(2)}) %collective-permute-start.9) | collective-permute-done | bytes 15392 | tf_op jit(solution)/shard_map/ppermute | solution.py:166
  61.2 0.6 gather_fusion
  61.8 0.1 copy.48
  61.8 0.1 reshape_reshape.7
  61.9 0.2 broadcast_select_fusion
  62.1 1.5 %fusion.51 = f32[30,32,128]{2,1,0:T(8,128)} fusion(f32[30,32,128]{2,1,0:T(8,128)S(1)} %bitcast.121, pred[32,1024]{1,0:T(8,128)(4,1)S(1)} %iota_compare_fusion.1, bf16[30,1024]{1,0:T(8,128)(2,1)S(1)} %bitcast.128, s32[1024]{0:T(1024)S(1)} %bitcast.138), kind=kOutput, calls=%fused_computation.65 | convolution fusion | flops 252895232 | bytes 1081344 | tf_op jit(solution)/shard_map/dot_general | solution.py:180
  (45 shorter events, 0.5 us)
Async XLA Ops:
  0.0 39.7 %copy-start = (bf16[1,120,1024]{2,1,0:T(8,128)(2,1)S(1)}, bf16[1,120,1024]{2,1,0:T(8,128)(2,1)}, u32[]{:S(2)}) copy-start(bf16[1,120,1024]{2,1,0:T(8,128)(2,1)} %param.11) | copy-start | bytes 737284
  1.1 5.8 %collective-permute-start.1 = (f32[45,3,128]{2,1,0:T(4,128)S(1)}, f32[45,3,128]{2,1,0:T(4,128)S(1)}, u32[]{:S(2)}, u32[]{:S(2)}) collective-permute-start(f32[45,3,128]{2,1,0:T(4,128)S(1)} %get-tuple-element.24), channel_id=1, source_target_pairs={{8,0},{16,8},{24,16},{9,1},{17,9},{25,17},{10,2},{18,10},{26,18},{... | collective-permute-start | bytes 207368 | tf_op jit(solution)/shard_map/ppermute | solution.py:26
  2.4 4.6 %collective-permute-start = (f32[45,3,128]{2,1,0:T(4,128)S(1)}, f32[45,3,128]{2,1,0:T(4,128)S(1)}, u32[]{:S(2)}, u32[]{:S(2)}) collective-permute-start(f32[45,3,128]{2,1,0:T(4,128)S(1)} %get-tuple-element.23), channel_id=1, source_target_pairs={{0,8},{8,16},{16,24},{1,9},{9,17},{17,25},{2,10},{10,18},{18,26},{... | collective-permute-start | bytes 207368 | tf_op jit(solution)/shard_map/ppermute | solution.py:23
  9.0 8.0 %copy-start.1 = (f32[2,15,32,128]{3,2,1,0:T(8,128)S(1)}, f32[2,15,32,128]{3,2,1,0:T(8,128)}, u32[]{:S(2)}) copy-start(f32[2,15,32,128]{3,2,1,0:T(8,128)} %param.7) | copy-start | bytes 1474564
  9.0 8.0 %copy-start.2 = (f32[15,32,128]{2,1,0:T(8,128)S(1)}, f32[15,32,128]{2,1,0:T(8,128)}, u32[]{:S(2)}) copy-start(f32[15,32,128]{2,1,0:T(8,128)} %param.8) | copy-start | bytes 737284
  9.5 6.6 %collective-permute-start.2 = (f32[45,38,6]{0,1,2:T(8,128)S(1)}, f32[45,38,6]{0,1,2:T(8,128)S(1)}, u32[]{:S(2)}, u32[]{:S(2)}) collective-permute-start(f32[45,38,6]{0,1,2:T(8,128)S(1)} %pad_maximum_fusion.14), channel_id=1, source_target_pairs={{0,4},{4,0},{1,5},{5,1},{2,6},{6,2},{3,7},{7,3},{8,12},{12,8},{9,1... | collective-permute-start | bytes 123128 | tf_op jit(solution)/shard_map/ppermute | solution.py:34
  23.5 8.2 %copy-start.3 = (s32[1,1024,1]{1,2,0:T(1,128)S(1)}, s32[1,1024,1]{1,2,0:T(1,128)}, u32[]{:S(2)}) copy-start(s32[1,1024,1]{1,2,0:T(1,128)} %param.10) | copy-start | bytes 12292
  25.0 14.5 %all-to-all-start = ((bf16[30,8,256]{2,0,1:T(8,128)(2,1)}), bf16[30,8,256]{2,0,1:T(8,128)(2,1)S(1)}, u32[]{:S(2)}, u32[]{:S(2)}) async-start(bf16[30,8,256]{2,0,1:T(8,128)(2,1)} %bitcast.6), calls=%async_computation | async-start | bytes 262144 | tf_op jit(solution)/shard_map/all_to_all | solution.py:148
  39.7 3.8 %copy-start.4 = (bf16[1,1024,120]{1,2,0:T(8,128)(2,1)S(1)}, bf16[1,1024,120]{1,2,0:T(8,128)(2,1)}, u32[]{:S(2)}) copy-start(bf16[1,1024,120]{1,2,0:T(8,128)(2,1)} %param.13) | copy-start | bytes 737284
  47.4 5.2 %collective-permute-start.3 = (bf16[30,1,256]{2,0,1:T(8,128)(2,1)S(1)}, bf16[30,1,256]{2,0,1:T(8,128)(2,1)S(1)}, u32[]{:S(2)}, u32[]{:S(2)}) collective-permute-start(bf16[30,1,256]{2,0,1:T(8,128)(2,1)S(1)} %bitcast.135), channel_id=1, source_target_pairs={{0,1},{1,0},{2,3},{3,2},{4,5},{5,4},{6,7},{7,6},{8,9},{9,8},{10,11... | collective-permute-start | bytes 46088 | tf_op jit(solution)/shard_map/ppermute | solution.py:166
  47.5 7.2 %collective-permute-start.4 = (bf16[30,1,256]{2,0,1:T(8,128)(2,1)S(1)}, bf16[30,1,256]{2,0,1:T(8,128)(2,1)S(1)}, u32[]{:S(2)}, u32[]{:S(2)}) collective-permute-start(bf16[30,1,256]{2,0,1:T(8,128)(2,1)S(1)} %bitcast.134), channel_id=1, source_target_pairs={{0,2},{1,3},{2,0},{3,1},{4,6},{5,7},{6,4},{7,5},{8,10},{9,11},{10,... | collective-permute-start | bytes 46088 | tf_op jit(solution)/shard_map/ppermute | solution.py:166
  48.5 10.3 %collective-permute-start.5 = (bf16[30,1,256]{2,0,1:T(8,128)(2,1)S(1)}, bf16[30,1,256]{2,0,1:T(8,128)(2,1)S(1)}, u32[]{:S(2)}, u32[]{:S(2)}) collective-permute-start(bf16[30,1,256]{2,0,1:T(8,128)(2,1)S(1)} %bitcast.133), channel_id=1, source_target_pairs={{0,3},{1,2},{2,1},{3,0},{4,7},{5,6},{6,5},{7,4},{8,11},{9,10},{10,... | collective-permute-start | bytes 46088 | tf_op jit(solution)/shard_map/ppermute | solution.py:166
  51.9 6.9 %collective-permute-start.6 = (bf16[30,1,256]{2,0,1:T(8,128)(2,1)S(1)}, bf16[30,1,256]{2,0,1:T(8,128)(2,1)S(1)}, u32[]{:S(2)}, u32[]{:S(2)}) collective-permute-start(bf16[30,1,256]{2,0,1:T(8,128)(2,1)S(1)} %bitcast.132), channel_id=1, source_target_pairs={{0,4},{1,5},{2,6},{3,7},{4,0},{5,1},{6,2},{7,3},{8,12},{9,13},{10,... | collective-permute-start | bytes 46088 | tf_op jit(solution)/shard_map/ppermute | solution.py:166
  52.5 6.3 %collective-permute-start.7 = (bf16[30,1,256]{2,0,1:T(8,128)(2,1)S(1)}, bf16[30,1,256]{2,0,1:T(8,128)(2,1)S(1)}, u32[]{:S(2)}, u32[]{:S(2)}) collective-permute-start(bf16[30,1,256]{2,0,1:T(8,128)(2,1)S(1)} %bitcast.131), channel_id=1, source_target_pairs={{0,5},{1,4},{2,7},{3,6},{4,1},{5,0},{6,3},{7,2},{8,13},{9,12},{10,... | collective-permute-start | bytes 46088 | tf_op jit(solution)/shard_map/ppermute | solution.py:166
  52.6 6.3 %collective-permute-start.8 = (bf16[30,1,256]{2,0,1:T(8,128)(2,1)S(1)}, bf16[30,1,256]{2,0,1:T(8,128)(2,1)S(1)}, u32[]{:S(2)}, u32[]{:S(2)}) collective-permute-start(bf16[30,1,256]{2,0,1:T(8,128)(2,1)S(1)} %bitcast.130), channel_id=1, source_target_pairs={{0,6},{1,7},{2,4},{3,5},{4,2},{5,3},{6,0},{7,1},{8,14},{9,15},{10,... | collective-permute-start | bytes 46088 | tf_op jit(solution)/shard_map/ppermute | solution.py:166
  54.8 6.4 %collective-permute-start.9 = (bf16[30,1,256]{2,0,1:T(8,128)(2,1)S(1)}, bf16[30,1,256]{2,0,1:T(8,128)(2,1)S(1)}, u32[]{:S(2)}, u32[]{:S(2)}) collective-permute-start(bf16[30,1,256]{2,0,1:T(8,128)(2,1)S(1)} %bitcast.129), channel_id=1, source_target_pairs={{0,7},{1,6},{2,5},{3,4},{4,3},{5,2},{6,1},{7,0},{8,15},{9,14},{10,... | collective-permute-start | bytes 46088 | tf_op jit(solution)/shard_map/ppermute | solution.py:166
